TPU v7x, 512 devices: a whole 4x8x8 slice. The times are simulated.
512 devices in a mesh: section: 2 (over core), req: 64 (over y, z), head: 4 (over x).
Axes of the slice: x: 4, y: 8, z: 8, core: 2. Of those that a mesh axis runs over, the one named last changes fastest.
Arguments:
- embedding_per_slot: bfloat16 [512, 4, 1024], P('req', None, 'head'), may hold values from -6 to 6
- tally_per_slot: int32 [512], P('req'), may hold values from 1 to 4
- slot_requests: int32 [512], replicated, may hold values from 0 to 511, as said below
- memory_per_request: float32 [2, 512, 16, 64, 64], P('section', 'req', 'head'), may hold values from -4 to 4
- previous_step_feature: bfloat16 [2, 512, 1024], P('section', 'req', 'head'), may hold values from -6 to 6
- lag_interpolants: bfloat16 [2, 5, 1024], P('section'), may hold values from 0 to 1
- acceptor_projection: bfloat16 [2, 1024, 1024], P('section', None, 'head'), may hold values from -0.1875 to 0.1875
- address_projection: bfloat16 [2, 1024, 1024], P('section', None, 'head'), may hold values from -0.1875 to 0.1875
- content_projection: bfloat16 [2, 1024, 1024], P('section', None, 'head'), may hold values from -0.1875 to 0.1875
- readout_projection: bfloat16 [2, 1024, 1024], P('section', 'head'), may hold values from -0.1875 to 0.1875
- fading_first_lowrank: bfloat16 [2, 1024, 96], P('section', 'head'), may hold values from -0.1875 to 0.1875
- fading_second_lowrank: bfloat16 [2, 96, 1024], P('section', None, 'head'), may hold values from -0.625 to 0.625
- adapt_first_lowrank: bfloat16 [2, 1024, 96], P('section', 'head'), may hold values from -0.1875 to 0.1875
- adapt_second_lowrank: bfloat16 [2, 96, 1024], P('section', None, 'head'), may hold values from -0.625 to 0.625
- fading_baseline: float32 [2, 1024], P('section', 'head'), may hold values from -4 to 1
- adapt_baseline: float32 [2, 1024], P('section', 'head'), may hold values from -3 to 3
- erasing_address_gains: float32 [2, 1024], P('section', 'head'), may hold values from 0.5 to 1.5
- address_rate_coupling: float32 [2, 1024], P('section', 'head'), may hold values from 0 to 1
- present_extra_gain: float32 [2, 1024], P('section', 'head'), may hold values from -3 to 3
- section_standard_gains: float32 [2, 1024], P('section', 'head'), may hold values from 0.1 to 1.9
- section_standard_shift_terms: float32 [2, 1024], P('section', 'head'), may hold values from -2 to 2
Outputs:
- layer_out: bfloat16 [2, 512, 4, 1024], P('section', 'req', None, 'head')
Inputs may be any that keep to these rules, and one draw needn't show every extreme that they name: `slot_requests`: every request appears once. Of one group's 8 arrival slots at most 1 hold requests stored in any one group, and each group holds exactly 1 from some group.
All inputs are finite; a program needn't handle non-finite values.
Results may differ from a plain program's by a relative error of at most 0.02.
Values may be sent and summed in bfloat16 or wider, within the bound.
No kernel may reach another device: no remote copies, remote signals or barrier semaphores. Data moves between devices by JAX's collectives and lax.ppermute only.
A program may use at most 64 MiB of HBM per device.

v0:
```python
import jax
import jax.numpy as jnp
from jax import lax
from jax.sharding import PartitionSpec as P

highest = lax.Precision.HIGHEST


def from_behind(block, axis, distance):
    devices = range(lax.axis_size(axis))
    route = [(i - distance, i) for i in devices if i - distance in devices]
    return lax.ppermute(block, axis, route)


def sequence_recurrence(
    acceptor_entries,
    address_entries,
    content_entries,
    latent_response,
    adapt_latent,
    starting_memory,
    fading_second_lowrank,
    adapt_second_lowrank,
    fading_baseline,
    adapt_baseline,
    erasing_address_gains,
    address_rate_coupling,
    present_extra_gain,
    section_standard_gains,
    section_standard_shift_terms,
):
    batch_rows = starting_memory.shape[0]
    stored_memory_parts = starting_memory.shape[1]
    subspace_span = starting_memory.shape[2]

    def to_heads(array_in):
        return array_in.reshape(batch_rows, -1, stored_memory_parts, subspace_span)

    log_rate = (
        -jax.nn.softplus(
            -(
                fading_baseline
                + jnp.dot(
                    latent_response, fading_second_lowrank, preferred_element_type=jnp.float32
                )
            )
        )
        - 0.5
    )
    decays = to_heads(jnp.exp(-jnp.exp(log_rate)))
    learning = jax.nn.sigmoid(
        adapt_baseline
        + jnp.dot(adapt_latent, adapt_second_lowrank, preferred_element_type=jnp.float32)
    )
    learn_heads = to_heads(learning)
    scaled = to_heads(address_entries * erasing_address_gains)
    normed = scaled / jnp.sqrt(jnp.sum(scaled * scaled, axis=-1, keepdims=True) + 1e-06)
    erasing_address = to_heads(address_entries * (1.0 + (learning - 1.0) * address_rate_coupling))
    acceptor_parts = to_heads(acceptor_entries)
    content_part_lines = to_heads(content_entries)
    states = starting_memory
    readout = []
    for position in range(acceptor_parts.shape[1]):
        pulled = jnp.einsum("rhij,rhj->rhi", states, normed[:, position], precision=highest)
        states = (
            states * decays[:, position][:, :, None, :]
            - jnp.einsum(
                "rhi,rhj->rhij",
                pulled,
                normed[:, position] * learn_heads[:, position],
                precision=highest,
            )
            + jnp.einsum(
                "rhi,rhj->rhij",
                content_part_lines[:, position],
                erasing_address[:, position],
                precision=highest,
            )
        )
        readout.append(
            jnp.einsum("rhij,rhj->rhi", states, acceptor_parts[:, position], precision=highest)
        )
    read_all = jnp.stack(readout, axis=1)
    center = read_all - jnp.mean(read_all, axis=-1, keepdims=True)
    variance = jnp.mean(center * center, axis=-1, keepdims=True)
    gain_heads = section_standard_gains.reshape(stored_memory_parts, subspace_span)
    bias_heads = section_standard_shift_terms.reshape(stored_memory_parts, subspace_span)
    standardized_parts = center / jnp.sqrt(variance + 0.00064) * gain_heads + bias_heads
    present_extra_term = (
        jnp.sum(
            acceptor_parts
            * erasing_address
            * present_extra_gain.reshape(stored_memory_parts, subspace_span),
            axis=-1,
            keepdims=True,
        )
        * content_part_lines
    )
    return (
        (standardized_parts + present_extra_term)
        .astype(jnp.bfloat16)
        .reshape(-1, stored_memory_parts * subspace_span)
    )


def run_sublevel(lowrank_latent, earlier_entry, starting_memory, params):
    (
        lag_interpolants,
        acceptor_projection,
        address_projection,
        content_projection,
        readout_projection,
        fading_first_lowrank,
        fading_second_lowrank,
        adapt_first_lowrank,
        adapt_second_lowrank,
        fading_baseline,
        adapt_baseline,
        erasing_address_gains,
        address_rate_coupling,
        present_extra_gain,
        section_standard_gains,
        section_standard_shift_terms,
    ) = params
    batch_rows, steps_count, shard_width = lowrank_latent.shape
    previous = jnp.concatenate([earlier_entry[:, None, :], lowrank_latent[:, :-1, :]], axis=1)
    piece_now = lax.all_gather(lowrank_latent, "head", axis=2, tiled=True)
    piece_prev = lax.all_gather(previous, "head", axis=2, tiled=True)
    span_width = piece_now.shape[2]
    coef_rows = lag_interpolants.astype(jnp.float32)
    current_piece = piece_now.astype(jnp.float32)
    spread_piece = piece_prev.astype(jnp.float32) - current_piece
    updated = []
    for slot_num, which_mix, weight_all in (
        (0, 0, acceptor_projection),
        (1, 2, address_projection),
        (2, 3, content_projection),
    ):
        blend = (
            (current_piece + spread_piece * coef_rows[which_mix])
            .astype(jnp.bfloat16)
            .reshape(-1, span_width)
        )
        updated.append(jnp.dot(blend, weight_all, preferred_element_type=jnp.float32))
    acceptor_entries = updated[0]
    address_entries = updated[1]
    content_entries = updated[2]
    current = lowrank_latent.astype(jnp.float32)
    spread = previous.astype(jnp.float32) - current
    column_start = lax.axis_index("head") * shard_width
    decay_mix = lax.dynamic_slice_in_dim(lag_interpolants[1], column_start, shard_width, 0).astype(
        jnp.float32
    )
    learn_mix = lax.dynamic_slice_in_dim(lag_interpolants[4], column_start, shard_width, 0).astype(
        jnp.float32
    )
    decay_input = (current + spread * decay_mix).astype(jnp.bfloat16).reshape(-1, shard_width)
    learn_input = (current + spread * learn_mix).astype(jnp.bfloat16).reshape(-1, shard_width)
    partial_rank = jnp.dot(decay_input, fading_first_lowrank, preferred_element_type=jnp.float32)
    partial_learn = jnp.dot(learn_input, adapt_first_lowrank, preferred_element_type=jnp.float32)
    decay_total, learn_total = lax.psum((partial_rank, partial_learn), "head")
    latent_response = jnp.tanh(decay_total).astype(jnp.bfloat16)
    adapt_latent = learn_total.astype(jnp.bfloat16)
    lagged_features = sequence_recurrence(
        acceptor_entries,
        address_entries,
        content_entries,
        latent_response,
        adapt_latent,
        starting_memory,
        fading_second_lowrank,
        adapt_second_lowrank,
        fading_baseline,
        adapt_baseline,
        erasing_address_gains,
        address_rate_coupling,
        present_extra_gain,
        section_standard_gains,
        section_standard_shift_terms,
    )
    own_rows = lax.psum_scatter(
        lax.dot_general(
            readout_projection,
            lagged_features,
            (((0,), (1,)), ((), ())),
            preferred_element_type=jnp.float32,
        ),
        "head",
        scatter_dimension=0,
        tiled=True,
    )
    projected = own_rows.T.reshape(batch_rows, steps_count, shard_width)
    return (current + projected).astype(jnp.bfloat16)


def run_sections(inputs, states_use, last_use, params):
    section_num = lax.axis_index("section")
    section_count = lax.axis_size("section")
    block_count = 1
    block_rows = inputs.shape[0] // block_count
    result = jnp.zeros_like(inputs)
    incoming = jnp.zeros((block_rows,) + inputs.shape[1:], jnp.bfloat16)
    tick_total = block_count + section_count - 1
    for tick_num in range(tick_total):
        lag = tick_num - section_num
        entering = jnp.where(section_num == 0, inputs, incoming)
        produced = run_sublevel(entering, last_use, states_use, params)
        is_valid = (lag >= 0) & (lag < block_count)
        result = jnp.where(is_valid, produced, result)
        if tick_num + 1 < tick_total:
            incoming = from_behind(produced, "section", 1)
    return result


def body(
    embedding_per_slot,
    tally_per_slot,
    slot_requests,
    memory_per_request,
    previous_step_feature,
    lag_interpolants,
    acceptor_projection,
    address_projection,
    content_projection,
    readout_projection,
    fading_first_lowrank,
    fading_second_lowrank,
    adapt_first_lowrank,
    adapt_second_lowrank,
    fading_baseline,
    adapt_baseline,
    erasing_address_gains,
    address_rate_coupling,
    present_extra_gain,
    section_standard_gains,
    section_standard_shift_terms,
):
    local_rows = embedding_per_slot.shape[0]
    groups = lax.axis_size("req")
    capacity = (local_rows + groups - 1) // groups
    my_group = lax.axis_index("req")
    slot_ids = jnp.arange(local_rows, dtype=jnp.int32)
    table = slot_requests.reshape(groups, local_rows)
    my_arrivals = lax.dynamic_index_in_dim(table, my_group, 0, keepdims=False)
    home_group = my_arrivals // local_rows
    earlier = slot_ids[None, :] < slot_ids[:, None]
    arrival_rank = jnp.sum(
        ((home_group[:, None] == home_group[None, :]) & earlier).astype(jnp.int32), axis=1
    )
    arrival_slot = home_group * capacity + arrival_rank
    requests = my_group * local_rows + slot_ids
    total_rows = slot_requests.shape[0]
    found = slot_requests[None, :] == requests[:, None]
    positions = jnp.sum(
        jnp.where(found, jnp.arange(total_rows, dtype=jnp.int32)[None, :], 0), axis=1
    )
    source = positions // local_rows
    within = positions % local_rows
    source_homes = jnp.take(table, source, axis=0) // local_rows
    home_rank = jnp.sum(
        ((source_homes == my_group) & (slot_ids[None, :] < within[:, None])).astype(jnp.int32),
        axis=1,
    )
    home_slot = source * capacity + home_rank
    buffer_rows = groups * capacity
    params = (
        lag_interpolants[0],
        acceptor_projection[0],
        address_projection[0],
        content_projection[0],
        readout_projection[0],
        fading_first_lowrank[0],
        fading_second_lowrank[0],
        adapt_first_lowrank[0],
        adapt_second_lowrank[0],
        fading_baseline[0],
        adapt_baseline[0],
        erasing_address_gains[0],
        address_rate_coupling[0],
        present_extra_gain[0],
        section_standard_gains[0],
        section_standard_shift_terms[0],
    )
    states_local = memory_per_request[0]
    last_local = previous_step_feature[0]
    outgoing = (
        jnp.zeros((buffer_rows,) + embedding_per_slot.shape[1:], jnp.bfloat16)
        .at[arrival_slot]
        .set(embedding_per_slot)
    )
    arrived = lax.all_to_all(outgoing, "req", split_axis=0, concat_axis=0, tiled=True)
    inputs = jnp.take(arrived, home_slot, axis=0)
    result = run_sections(inputs, states_local, last_local, params)
    going_back = (
        jnp.zeros((buffer_rows,) + result.shape[1:], jnp.bfloat16).at[home_slot].set(result)
    )
    returned = lax.all_to_all(going_back, "req", split_axis=0, concat_axis=0, tiled=True)
    result = jnp.take(returned, arrival_slot, axis=0)
    live_mask = (
        jnp.arange(embedding_per_slot.shape[1], dtype=jnp.int32)[None, :] < tally_per_slot[:, None]
    )
    return jnp.where(live_mask[:, :, None], result, jnp.zeros_like(result))[None]


def solution(mesh):
    return jax.shard_map(
        body,
        mesh=mesh,
        in_specs=(
            P("req", None, "head"),
            P("req"),
            P(),
            P("section", "req", "head", None, None),
            P("section", "req", "head"),
            P("section", None, None),
            P("section", None, "head"),
            P("section", None, "head"),
            P("section", None, "head"),
            P("section", "head", None),
            P("section", "head", None),
            P("section", None, "head"),
            P("section", "head", None),
            P("section", None, "head"),
            P("section", "head"),
            P("section", "head"),
            P("section", "head"),
            P("section", "head"),
            P("section", "head"),
            P("section", "head"),
            P("section", "head"),
        ),
        out_specs=P("section", "req", None, "head"),
        check_vma=False,
    )
```

profile of v0, /device:TPU:8, one launch (start us, length us, event | category | flops | bytes accessed | tf_op | source)
XLA Modules:
  0.0 273.9 jit_solution(2103046319629629872)
XLA Ops:
  8.4 2.0 scatter_fusion
  10.3 16.6 %all-to-all-start = ((bf16[64,4,256]{2,1,0:T(4,128)(2,1)}), bf16[64,4,256]{2,1,0:T(4,128)(2,1)S(1)}, u32[]{:S(2)}, u32[]{:S(2)}) async-start(bf16[64,4,256]{2,1,0:T(4,128)(2,1)} %scatter_fusion), calls=%async_computation | async-start | bytes 262144 | tf_op jit(solution)/shard_map/all_to_all | solution.py:291
  36.4 2.2 all-to-all-done
  39.2 12.3 %all_gather.12 = bf16[8,4,1024]{2,0,1:T(8,128)(2,1)S(1)} all-gather(bf16[8,4,256]{2,0,1:T(8,128)(2,1)S(1)} %broadcast_select_fusion.1), channel_id=1, replica_groups=mesh['section'=2,'req'=64,'head'=4] {'head'}, dimensions={2}, use_global_device_ids=true | all-gather | bytes 81920 | tf_op jit(solution)/shard_map/all_gather | solution.py:127
  51.5 11.9 %all_gather.13 = bf16[8,4,1024]{2,0,1:T(8,128)(2,1)S(1)} all-gather(bf16[8,4,256]{2,0,1:T(8,128)(2,1)S(1)} %pad_maximum_fusion.3), channel_id=1, replica_groups=mesh['section'=2,'req'=64,'head'=4] {'head'}, dimensions={2}, use_global_device_ids=true | all-gather | bytes 81920 | tf_op jit(solution)/shard_map/all_gather | solution.py:128
  65.4 16.7 %all-reduce.1 = (bf16[32,96]{1,0:T(8,128)(2,1)S(1)}, f32[32,96]{1,0:T(8,128)S(1)}) all-reduce(f32[32,96]{1,0:T(8,128)S(1)} %fusion.86, f32[32,96]{1,0:T(8,128)S(1)} %fusion.92), channel_id=1, replica_groups=mesh['section'=2,'req'=64,'head'=4] {'head'}, use_global_device_ids=true, to_apply=%region_6.8 | all-reduce | flops 6144 | bytes 43008 | tf_op jit(solution)/shard_map/psum | solution.py:161
  92.2 1.7 fusion.20
  93.9 2.1 fusion.137
  96.7 2.1 fusion.160
  99.6 3.2 %fusion.55 = f32[8,4,1,64]{3,2,1,0:T(1,128)S(1)} fusion(f32[8,4,64]{2,1,0:T(4,128)S(1)} %copy-done.15, f32[8,4,64]{2,1,0:T(4,128)S(1)} %copy.164, f32[8,4,64]{2,1,0:T(4,128)S(1)} %copy-done.9, f32[8,4,64]{2,1,0:T(4,128)S(1)} %bitcast.461, f32[8,4,64]{2,1,0:T(4,128)S(1)} %get-tuple-element.50, f32[8,4,64,1]{2,0,1,3:T(8,128)S(1)} %copy-done.31, ...), kind=kOutput, calls=%fused_computation.72 | convolution fusion | flops 2883584 | bytes 622592 | tf_op jit(solution)/shard_map/rhij,rhj->rhi/dot_general | solution.py:81
  103.5 2.8 %fusion.54 = f32[8,4,1,64]{3,2,1,0:T(1,128)S(1)} fusion(f32[8,4,64,1]{2,3,1,0:T(1,128)S(1)} %bitcast.471, f32[8,4,64]{2,1,0:T(4,128)S(1)} %copy-done.15, f32[8,4,64]{2,1,0:T(4,128)S(1)} %copy.164, f32[8,4,64]{2,1,0:T(4,128)S(1)} %copy-done.9, f32[8,4,64]{2,1,0:T(4,128)S(1)} %bitcast.462, f32[8,4,64]{2,1,0:T(4,128)S(1)} %get-tuple-element.50, ...), kind=kOutput, calls=%fused_computation.71 | convolution fusion | flops 2883584 | bytes 622592 | tf_op jit(solution)/shard_map/rhij,rhj->rhi/dot_general | solution.py:64
  107.0 2.0 multiply_add_fusion.2
  109.1 1.7 fusion.134
  111.5 1.7 fusion.168
  114.0 2.1 fusion.32
  118.4 22.9 %reduce-scatter.3.cloned.1.call-done = f32[256,32]{0,1:T(8,128)} async-done(((f32[1024,32]{0,1:T(8,128)}), f32[256,32]{0,1:T(8,128)}) %reduce-scatter.3.cloned.1.call-update) | async-done | bytes 32784 | tf_op jit(solution)/shard_map/reduce_scatter | solution.py:181
  144.3 12.0 %all_gather.14 = bf16[8,4,1024]{2,0,1:T(8,128)(2,1)S(1)} all-gather(bf16[8,4,256]{2,0,1:T(8,128)(2,1)S(1)} %broadcast_select_fusion), channel_id=1, replica_groups=mesh['section'=2,'req'=64,'head'=4] {'head'}, dimensions={2}, use_global_device_ids=true | all-gather | bytes 81920 | tf_op jit(solution)/shard_map/all_gather | solution.py:127
  156.4 11.9 %all_gather.15 = bf16[8,4,1024]{2,0,1:T(8,128)(2,1)S(1)} all-gather(bf16[8,4,256]{2,0,1:T(8,128)(2,1)S(1)} %pad_maximum_fusion.2), channel_id=1, replica_groups=mesh['section'=2,'req'=64,'head'=4] {'head'}, dimensions={2}, use_global_device_ids=true | all-gather | bytes 81920 | tf_op jit(solution)/shard_map/all_gather | solution.py:128
  171.8 15.1 %all-reduce = (bf16[32,96]{1,0:T(8,128)(2,1)S(1)}, f32[32,96]{1,0:T(8,128)S(1)}) all-reduce(f32[32,96]{1,0:T(8,128)S(1)} %fusion.84, f32[32,96]{1,0:T(8,128)S(1)} %fusion.90), channel_id=1, replica_groups=mesh['section'=2,'req'=64,'head'=4] {'head'}, use_global_device_ids=true, to_apply=%region_13.15 | all-reduce | flops 6144 | bytes 43008 | tf_op jit(solution)/shard_map/psum | solution.py:161
  189.1 1.7 fusion.18
  192.1 2.1 fusion.131
  194.1 2.1 fusion.155
  196.2 3.2 %fusion.57 = f32[8,4,1,64]{3,2,1,0:T(1,128)S(1)} fusion(f32[8,4,64]{2,1,0:T(4,128)S(1)} %get-tuple-element.42, f32[8,4,64]{2,1,0:T(4,128)S(1)} %copy.178, f32[8,4,64]{2,1,0:T(4,128)S(1)} %get-tuple-element.18, f32[8,4,64]{2,1,0:T(4,128)S(1)} %bitcast.464, f32[8,4,64]{2,1,0:T(4,128)S(1)} %get-tuple-element.30, f32[8,4,64,1]{2,0,1,3:T(8,128)S(1)} %get-tuple-element.27, ...), kind=kOutput, calls=%fused_computation.74 | convolution fusion | flops 2883584 | bytes 622592 | tf_op jit(solution)/shard_map/rhij,rhj->rhi/dot_general | solution.py:81
  199.5 2.8 %fusion.56 = f32[8,4,1,64]{3,2,1,0:T(1,128)S(1)} fusion(f32[8,4,64,1]{2,3,1,0:T(1,128)S(1)} %bitcast.473, f32[8,4,64]{2,1,0:T(4,128)S(1)} %get-tuple-element.42, f32[8,4,64]{2,1,0:T(4,128)S(1)} %copy.178, f32[8,4,64]{2,1,0:T(4,128)S(1)} %get-tuple-element.18, f32[8,4,64]{2,1,0:T(4,128)S(1)} %bitcast.465, f32[8,4,64]{2,1,0:T(4,128)S(1)} %get-tuple-element.30, ...), kind=kOutput, calls=%fused_computation.73 | convolution fusion | flops 2883584 | bytes 622592 | tf_op jit(solution)/shard_map/rhij,rhj->rhi/dot_general | solution.py:64
  202.3 2.0 multiply_add_fusion
  204.3 1.7 fusion.128
  206.1 1.7 fusion.169
  207.8 2.1 fusion.26
  213.6 23.6 %reduce-scatter.5.cloned.1.call-done = f32[256,32]{0,1:T(8,128)} async-done(((f32[1024,32]{0,1:T(8,128)}), f32[256,32]{0,1:T(8,128)}) %reduce-scatter.5.cloned.1.call-update) | async-done | bytes 32784 | tf_op jit(solution)/shard_map/reduce_scatter | solution.py:181
  238.7 1.9 scatter_fusion.1
  240.6 13.4 %all-to-all-start.1 = ((bf16[64,4,256]{2,1,0:T(4,128)(2,1)}), bf16[64,4,256]{2,1,0:T(4,128)(2,1)S(1)}, u32[]{:S(2)}, u32[]{:S(2)}) async-start(bf16[64,4,256]{2,1,0:T(4,128)(2,1)} %scatter_fusion.1), calls=%async_computation.3 | async-start | bytes 262144 | tf_op jit(solution)/shard_map/all_to_all | solution.py:297
  254.7 11.1 %all-to-all-done.1 = bf16[64,4,256]{2,1,0:T(4,128)(2,1)S(1)} async-done(((bf16[64,4,256]{2,1,0:T(4,128)(2,1)}), bf16[64,4,256]{2,1,0:T(4,128)(2,1)S(1)}, u32[]{:S(2)}, u32[]{:S(2)}) %all-to-all-start.1) | async-done | bytes 131104 | tf_op jit(solution)/shard_map/all_to_all | solution.py:297
  (268 shorter events, 47.0 us)
Async XLA Ops:
  6.5 111.0 %copy-start = (bf16[1,256,1024]{2,1,0:T(8,128)(2,1)S(1)}, bf16[1,256,1024]{2,1,0:T(8,128)(2,1)}, u32[]{:S(2)}) copy-start(bf16[1,256,1024]{2,1,0:T(8,128)(2,1)} %param.32) | copy-start | bytes 1572868
  6.5 23.3 %copy-start.3 = (bf16[1,1024,256]{2,1,0:T(8,128)(2,1)S(1)}, bf16[1,1024,256]{2,1,0:T(8,128)(2,1)}, u32[]{:S(2)}) copy-start(bf16[1,1024,256]{2,1,0:T(8,128)(2,1)} %param.29) | copy-start | bytes 1572868
  7.4 20.9 %copy-start.8 = (s32[64,8]{1,0:T(8,128)}, s32[64,8]{1,0:T(8,128)S(1)}, u32[]{:S(2)}) copy-start(s32[64,8]{1,0:T(8,128)S(1)} %reshape.364) | copy-start | bytes 6148
  10.3 28.2 %all-to-all-start = ((bf16[64,4,256]{2,1,0:T(4,128)(2,1)}), bf16[64,4,256]{2,1,0:T(4,128)(2,1)S(1)}, u32[]{:S(2)}, u32[]{:S(2)}) async-start(bf16[64,4,256]{2,1,0:T(4,128)(2,1)} %scatter_fusion), calls=%async_computation | async-start | bytes 262144 | tf_op jit(solution)/shard_map/all_to_all | solution.py:291
  26.9 114.4 %reduce-scatter.3.cloned.1.call-start = ((), (), s32[]{:S(2)}) async-start(), calls=%async_computation.4 | async-start | bytes 163840 | tf_op jit(solution)/shard_map/reduce_scatter | solution.py:181
  28.9 0.8 copy-start.25
  29.7 33.8 %copy-start.33 = (pred[8]{0:T(512)(128)(4,1)}, pred[8]{0:T(512)(128)(4,1)S(1)}, u32[]{:S(2)}) copy-start(pred[8]{0:T(512)(128)(4,1)S(1)} %get-tuple-element.12) | copy-start | bytes 28
  29.8 33.8 %copy-start.35 = (f32[1,1,256]{2,1,0:T(1,128)}, f32[1,1,256]{2,1,0:T(1,128)S(1)}, u32[]{:S(2)}) copy-start(f32[1,1,256]{2,1,0:T(1,128)S(1)} %get-tuple-element.77) | copy-start | bytes 3076
  29.8 33.8 %copy-start.37 = (f32[1,1,256]{2,1,0:T(1,128)}, f32[1,1,256]{2,1,0:T(1,128)S(1)}, u32[]{:S(2)}) copy-start(f32[1,1,256]{2,1,0:T(1,128)S(1)} %get-tuple-element.78) | copy-start | bytes 3076
  29.8 1.0 copy-start.4
  36.4 27.0 %copy-start.23 = (f32[1,1,1024]{2,1,0:T(1,128)}, f32[1,1,1024]{2,1,0:T(1,128)S(1)}, u32[]{:S(2)}) copy-start(f32[1,1,1024]{2,1,0:T(1,128)S(1)} %get-tuple-element.73) | copy-start | bytes 12292
  36.4 49.2 %copy-start.21 = (f32[1,1,1024]{2,1,0:T(1,128)}, f32[1,1,1024]{2,1,0:T(1,128)S(1)}, u32[]{:S(2)}) copy-start(f32[1,1,1024]{2,1,0:T(1,128)S(1)} %get-tuple-element.72) | copy-start | bytes 12292
  39.2 12.3 %copy-start.17 = (bf16[1,8,256]{2,1,0:T(8,128)(2,1)S(1)}, bf16[1,8,256]{2,1,0:T(8,128)(2,1)}, u32[]{:S(2)}) copy-start(bf16[1,8,256]{2,1,0:T(8,128)(2,1)} %param.27) | copy-start | bytes 12292
  63.4 19.7 %copy-start.2 = (bf16[1,1024,256]{2,1,0:T(8,128)(2,1)S(1)}, bf16[1,1024,256]{2,1,0:T(8,128)(2,1)}, u32[]{:S(2)}) copy-start(bf16[1,1024,256]{2,1,0:T(8,128)(2,1)} %param.30) | copy-start | bytes 1572868
  63.6 0.8 copy-start.5
  64.5 0.8 copy-start.6
  65.2 16.9 %copy-start.55 = (bf16[1,96,256]{2,1,0:T(8,128)(2,1)S(1)}, bf16[1,96,256]{2,1,0:T(8,128)(2,1)}, u32[]{:S(2)}) copy-start(bf16[1,96,256]{2,1,0:T(8,128)(2,1)} %param.36) | copy-start | bytes 147460
  85.6 5.9 %copy-start.1 = (f32[1,8,4,64,64]{4,3,2,1,0:T(8,128)S(1)}, f32[1,8,4,64,64]{4,3,2,1,0:T(8,128)}, u32[]{:S(2)}) copy-start(f32[1,8,4,64,64]{4,3,2,1,0:T(8,128)} %param.26) | copy-start | bytes 1572868
  92.2 1.7 copy-start.10
  92.2 1.7 copy-start.16
  92.2 1.8 copy-start.32
  96.7 2.1 copy-start.31
  107.0 2.0 copy-start.12
  111.5 1.8 copy-start.28
  118.4 118.8 %reduce-scatter.5.cloned.1.call-start = ((), (), s32[]{:S(2)}) async-start(), calls=%async_computation.5 | async-start | bytes 163840 | tf_op jit(solution)/shard_map/reduce_scatter | solution.py:181
  142.1 2.1 collective-permute-start
  144.3 12.0 %copy-start.18 = (bf16[1,8,256]{2,1,0:T(8,128)(2,1)S(1)}, bf16[1,8,256]{2,1,0:T(8,128)(2,1)}, u32[]{:S(2)}) copy-start(bf16[1,8,256]{2,1,0:T(8,128)(2,1)} %param.27) | copy-start | bytes 12292
  156.4 11.9 %copy-start.22 = (f32[1,1,1024]{2,1,0:T(1,128)S(1)}, f32[1,1,1024]{2,1,0:T(1,128)}, u32[]{:S(2)}) copy-start(f32[1,1,1024]{2,1,0:T(1,128)} %copy-done.21) | copy-start | bytes 12292
  170.9 0.8 copy-start.7
  171.7 15.3 %copy-start.56 = (bf16[1,96,256]{2,1,0:T(8,128)(2,1)S(1)}, bf16[1,96,256]{2,1,0:T(8,128)(2,1)}, u32[]{:S(2)}) copy-start(bf16[1,96,256]{2,1,0:T(8,128)(2,1)} %param.36) | copy-start | bytes 147460
  190.9 0.8 copy-start.57
  240.6 25.1 %all-to-all-start.1 = ((bf16[64,4,256]{2,1,0:T(4,128)(2,1)}), bf16[64,4,256]{2,1,0:T(4,128)(2,1)S(1)}, u32[]{:S(2)}, u32[]{:S(2)}) async-start(bf16[64,4,256]{2,1,0:T(4,128)(2,1)} %scatter_fusion.1), calls=%async_computation.3 | async-start | bytes 262144 | tf_op jit(solution)/shard_map/all_to_all | solution.py:297
  (36 other events, 24.8 us)
Sparse Core Ops, SparseCore 0:
  118.5 22.7 reduce-scatter.2
  211.7 25.4 reduce-scatter.4
where the time goes:
time: 276 us; the launch traced here: 274 us
  blocking collectives  80 us (29%)
  waiting for transfers between devices  60.6 us (22%)
  matrix products  40.9 us (15%)
  local copies, waits for them, and re-layouts  35.8 us (13%)
  starting transfers between devices  31.3 us (11%)
  between operations  14.4 us (5%)
  other arithmetic  11 us (4%)
    reduce_scatter x2, waiting for transfers between devices, run_sublevel(): lax.psum_scatter(lax.dot_general(readout_projection, lagged_features, (((...  46.5 us
    psum x2, blocking collectives, run_sublevel(): decay_total, learn_total = lax.psum((partial_rank, partial_learn), 'head')  31.9 us
    all_gather x2, blocking collectives, run_sublevel(): piece_now = lax.all_gather(lowrank_latent, 'head', axis=2, tiled=True)  24.4 us
    all_gather x2, blocking collectives, run_sublevel(): piece_prev = lax.all_gather(previous, 'head', axis=2, tiled=True)  23.7 us
    unnamed x129, local copies, waits for them, and re-layouts  19.1 us
    dot_general x8, matrix products, sequence_recurrence(): jnp.einsum('rhij,rhj->rhi', states, acceptor_parts[:, position], precisio...  18.2 us
    dot_general x8, matrix products, sequence_recurrence(): jnp.einsum('rhij,rhj->rhi', states, normed[:, position], precision=highest)  16.7 us
    all_to_all x1, starting transfers between devices, body(): lax.all_to_all(outgoing, 'req', split_axis=0, concat_axis=0, tiled=True)  16.6 us
  transfers between devices with their start and end apart: 5, of which 5 were waited for; matrix products, arithmetic and copies ran while one was open for 3% of the time, Pallas kernels for 0%

commit v1 on v0

--- a/solution.py
+++ b/solution.py
@@ -125,7 +125,16 @@
     batch_rows, steps_count, shard_width = lowrank_latent.shape
     previous = jnp.concatenate([earlier_entry[:, None, :], lowrank_latent[:, :-1, :]], axis=1)
     piece_now = lax.all_gather(lowrank_latent, "head", axis=2, tiled=True)
-    piece_prev = lax.all_gather(previous, "head", axis=2, tiled=True)
+    ways = lax.axis_size("head")
+    up = [(d, (d + 1) % ways) for d in range(ways)]
+    down = [(d, (d - 1) % ways) for d in range(ways)]
+    earlier_2, later = ([previous], [previous])
+    for _ in range(ways // 2):
+        earlier_2.append(lax.ppermute(earlier_2[-1], "head", up))
+    for _ in range((ways - 1) // 2):
+        later.append(lax.ppermute(later[-1], "head", down))
+    line = jnp.concatenate([*earlier_2[::-1], *later[1:]], axis=2)
+    piece_prev = jnp.roll(line, (lax.axis_index("head") - ways // 2) * previous.shape[2], axis=2)
     span_width = piece_now.shape[2]
     coef_rows = lag_interpolants.astype(jnp.float32)
     current_piece = piece_now.astype(jnp.float32)

time: 276 us -> 270 us (0.978)
  blocking collectives: 80 us -> 54.3 us
  starting transfers between devices: 31.3 us -> 50.2 us
  waiting for transfers between devices: 60.6 us -> 63.4 us
    all_gather x2 -> x0, blocking collectives: 23.7 us -> none  [run_sublevel(): piece_prev = lax.all_gather(previous, 'head', axis=2, tiled=True)]
    ppermute x0 -> x6, starting transfers between devices: none -> 18.9 us  [the longest x4 10.1 us: run_sublevel(): earlier_2.append(lax.ppermute(earlier_2[-1], 'head', up))]
    unnamed x129 -> x111, local copies, waits for them, and re-layouts: 19.1 us -> 17.1 us
  transfers between devices with their start and end apart: 5 -> 11, of which waited for: 5 -> 5; matrix products, arithmetic and copies ran while one was open for 3% -> 4% of each run, Pallas kernels for 0% -> 0%
where the time goes in v1:
time: 270 us; the launch traced here: 268 us
  waiting for transfers between devices  63.4 us (23%)
  blocking collectives  54.3 us (20%)
  starting transfers between devices  50.2 us (19%)
  matrix products  40.1 us (15%)
  local copies, waits for them, and re-layouts  34 us (13%)
  between operations  14.5 us (5%)
  other arithmetic  11.3 us (4%)
    reduce_scatter x2, waiting for transfers between devices, run_sublevel(): lax.psum_scatter(lax.dot_general(readout_projection, lagged_features, (((...  48.6 us
    psum x2, blocking collectives, run_sublevel(): decay_total, learn_total = lax.psum((partial_rank, partial_learn), 'head')  30.3 us
    all_gather x2, blocking collectives, run_sublevel(): piece_now = lax.all_gather(lowrank_latent, 'head', axis=2, tiled=True)  23.9 us
    dot_general x8, matrix products, sequence_recurrence(): jnp.einsum('rhij,rhj->rhi', states, acceptor_parts[:, position], precisio...  18.2 us
    unnamed x111, local copies, waits for them, and re-layouts  17.1 us
    dot_general x8, matrix products, sequence_recurrence(): jnp.einsum('rhij,rhj->rhi', states, normed[:, position], precision=highest)  16.8 us
    all_to_all x1, starting transfers between devices, body(): lax.all_to_all(outgoing, 'req', split_axis=0, concat_axis=0, tiled=True)  16.6 us
    all_to_all x1, starting transfers between devices, body(): lax.all_to_all(going_back, 'req', split_axis=0, concat_axis=0, tiled=True)  13.3 us
  transfers between devices with their start and end apart: 11, of which 5 were waited for; matrix products, arithmetic and copies ran while one was open for 4% of the time, Pallas kernels for 0%

profile of v1, /device:TPU:8, one launch (start us, length us, event | category | flops | bytes accessed | tf_op | source)
XLA Modules:
  0.0 267.8 jit_solution(7037447072947815110)
XLA Ops:
  8.9 2.0 scatter_fusion
  10.9 16.6 %all-to-all-start = ((bf16[64,4,256]{2,1,0:T(4,128)(2,1)}), bf16[64,4,256]{2,1,0:T(4,128)(2,1)S(1)}, u32[]{:S(2)}, u32[]{:S(2)}) async-start(bf16[64,4,256]{2,1,0:T(4,128)(2,1)} %scatter_fusion), calls=%async_computation | async-start | bytes 262144 | tf_op jit(solution)/shard_map/all_to_all | solution.py:300
  36.3 2.8 %all-to-all-done = bf16[64,4,256]{2,1,0:T(4,128)(2,1)S(1)} async-done(((bf16[64,4,256]{2,1,0:T(4,128)(2,1)}), bf16[64,4,256]{2,1,0:T(4,128)(2,1)S(1)}, u32[]{:S(2)}, u32[]{:S(2)}) %all-to-all-start) | async-done | bytes 131104 | tf_op jit(solution)/shard_map/all_to_all | solution.py:300
  40.4 3.4 %collective-permute-start = (bf16[8,4,256]{2,0,1:T(8,128)(2,1)S(1)}, bf16[8,4,256]{2,0,1:T(8,128)(2,1)S(1)}, u32[]{:S(2)}, u32[]{:S(2)}) collective-permute-start(bf16[8,4,256]{2,0,1:T(8,128)(2,1)S(1)} %pad_maximum_fusion.3), channel_id=1, source_target_pairs={{0,1},{1,2},{2,3},{3,0},{4,5},{5,6},{6,7},{7,4},{8,9},{9,10},{10,1... | collective-permute-start | bytes 49160 | tf_op jit(solution)/shard_map/ppermute | solution.py:133
  43.8 3.7 %collective-permute-start.2 = (bf16[8,4,256]{2,0,1:T(8,128)(2,1)S(1)}, bf16[8,4,256]{2,0,1:T(8,128)(2,1)S(1)}, u32[]{:S(2)}, u32[]{:S(2)}) collective-permute-start(bf16[8,4,256]{2,0,1:T(8,128)(2,1)S(1)} %pad_maximum_fusion.3), channel_id=1, source_target_pairs={{0,3},{1,0},{2,1},{3,2},{4,7},{5,4},{6,5},{7,6},{8,11},{9,8},{10,9... | collective-permute-start | bytes 49160 | tf_op jit(solution)/shard_map/ppermute | solution.py:135
  49.3 15.9 %all-reduce.1 = (bf16[32,96]{1,0:T(8,128)(2,1)S(1)}, f32[32,96]{1,0:T(8,128)S(1)}) all-reduce(f32[32,96]{1,0:T(8,128)S(1)} %fusion.104, f32[32,96]{1,0:T(8,128)S(1)} %fusion.110), channel_id=1, replica_groups=mesh['section'=2,'req'=64,'head'=4] {'head'}, use_global_device_ids=true, to_apply=%region_6.9 | all-reduce | flops 6144 | bytes 43008 | tf_op jit(solution)/shard_map/psum | solution.py:170
  67.7 1.9 collective-permute-start.1
  69.6 12.0 %all_gather.6 = bf16[8,4,1024]{2,0,1:T(8,128)(2,1)S(1)} all-gather(bf16[8,4,256]{2,0,1:T(8,128)(2,1)S(1)} %broadcast_select_fusion.1), channel_id=1, replica_groups=mesh['section'=2,'req'=64,'head'=4] {'head'}, dimensions={2}, use_global_device_ids=true | all-gather | bytes 81920 | tf_op jit(solution)/shard_map/all_gather | solution.py:127
  90.7 2.1 fusion.155
  93.5 2.1 fusion.180
  96.3 3.2 %fusion.55 = f32[8,4,1,64]{3,2,1,0:T(1,128)S(1)} fusion(f32[8,4,64]{2,1,0:T(4,128)S(1)} %get-tuple-element.67, f32[8,4,64]{2,1,0:T(4,128)S(1)} %copy.164, f32[8,4,64]{2,1,0:T(4,128)S(1)} %get-tuple-element.27, f32[8,4,64]{2,1,0:T(4,128)S(1)} %bitcast.463, f32[8,4,64]{2,1,0:T(4,128)S(1)} %copy-done.11, f32[8,4,64,1]{2,0,1,3:T(8,128)S(1)} %copy-done.19, ...), kind=kOutput, calls=%fused_computation.72 | convolution fusion | flops 2883584 | bytes 622592 | tf_op jit(solution)/shard_map/rhij,rhj->rhi/dot_general | solution.py:81
  100.3 2.8 %fusion.54 = f32[8,4,1,64]{3,2,1,0:T(1,128)S(1)} fusion(f32[8,4,64,1]{2,3,1,0:T(1,128)S(1)} %bitcast.473, f32[8,4,64]{2,1,0:T(4,128)S(1)} %get-tuple-element.67, f32[8,4,64]{2,1,0:T(4,128)S(1)} %copy.164, f32[8,4,64]{2,1,0:T(4,128)S(1)} %get-tuple-element.27, f32[8,4,64]{2,1,0:T(4,128)S(1)} %bitcast.464, f32[8,4,64]{2,1,0:T(4,128)S(1)} %copy-done.11, ...), kind=kOutput, calls=%fused_computation.71 | convolution fusion | flops 2883584 | bytes 622592 | tf_op jit(solution)/shard_map/rhij,rhj->rhi/dot_general | solution.py:64
  103.8 2.0 multiply_add_fusion.2
  107.6 1.7 fusion.190
  110.1 2.1 fusion.32
  114.5 23.9 %reduce-scatter.3.cloned.1.call-done = f32[256,32]{0,1:T(8,128)} async-done(((f32[1024,32]{0,1:T(8,128)}), f32[256,32]{0,1:T(8,128)}) %reduce-scatter.3.cloned.1.call-update) | async-done | bytes 32784 | tf_op jit(solution)/shard_map/reduce_scatter | solution.py:190
  141.4 2.1 collective-permute-start.4
  143.6 5.1 %collective-permute-start.6 = (bf16[8,4,256]{2,0,1:T(8,128)(2,1)S(1)}, bf16[8,4,256]{2,0,1:T(8,128)(2,1)S(1)}, u32[]{:S(2)}, u32[]{:S(2)}) collective-permute-start(bf16[8,4,256]{2,0,1:T(8,128)(2,1)S(1)} %pad_maximum_fusion.2), channel_id=1, source_target_pairs={{0,3},{1,0},{2,1},{3,2},{4,7},{5,4},{6,5},{7,6},{8,11},{9,8},{10,9... | collective-permute-start | bytes 49160 | tf_op jit(solution)/shard_map/ppermute | solution.py:135
  149.9 14.5 %all-reduce = (bf16[32,96]{1,0:T(8,128)(2,1)S(1)}, f32[32,96]{1,0:T(8,128)S(1)}) all-reduce(f32[32,96]{1,0:T(8,128)S(1)} %fusion.102, f32[32,96]{1,0:T(8,128)S(1)} %fusion.108), channel_id=1, replica_groups=mesh['section'=2,'req'=64,'head'=4] {'head'}, use_global_device_ids=true, to_apply=%region_13.16 | all-reduce | flops 6144 | bytes 43008 | tf_op jit(solution)/shard_map/psum | solution.py:170
  166.2 2.7 collective-permute-start.5
  168.9 11.9 %all_gather.7 = bf16[8,4,1024]{2,0,1:T(8,128)(2,1)S(1)} all-gather(bf16[8,4,256]{2,0,1:T(8,128)(2,1)S(1)} %broadcast_select_fusion), channel_id=1, replica_groups=mesh['section'=2,'req'=64,'head'=4] {'head'}, dimensions={2}, use_global_device_ids=true | all-gather | bytes 81920 | tf_op jit(solution)/shard_map/all_gather | solution.py:127
  185.0 2.1 fusion.149
  187.1 2.1 fusion.175
  189.2 3.2 %fusion.57 = f32[8,4,1,64]{3,2,1,0:T(1,128)S(1)} fusion(f32[8,4,64]{2,1,0:T(4,128)S(1)} %get-tuple-element.47, f32[8,4,64]{2,1,0:T(4,128)S(1)} %copy.178, f32[8,4,64]{2,1,0:T(4,128)S(1)} %get-tuple-element.23, f32[8,4,64]{2,1,0:T(4,128)S(1)} %bitcast.466, f32[8,4,64]{2,1,0:T(4,128)S(1)} %get-tuple-element.35, f32[8,4,64,1]{2,0,1,3:T(8,128)S(1)} %get-tuple-element.32, ...), kind=kOutput, calls=%fused_computation.74 | convolution fusion | flops 2883584 | bytes 622592 | tf_op jit(solution)/shard_map/rhij,rhj->rhi/dot_general | solution.py:81
  192.4 2.8 %fusion.56 = f32[8,4,1,64]{3,2,1,0:T(1,128)S(1)} fusion(f32[8,4,64,1]{2,3,1,0:T(1,128)S(1)} %bitcast.474, f32[8,4,64]{2,1,0:T(4,128)S(1)} %get-tuple-element.47, f32[8,4,64]{2,1,0:T(4,128)S(1)} %copy.178, f32[8,4,64]{2,1,0:T(4,128)S(1)} %get-tuple-element.23, f32[8,4,64]{2,1,0:T(4,128)S(1)} %bitcast.467, f32[8,4,64]{2,1,0:T(4,128)S(1)} %get-tuple-element.35, ...), kind=kOutput, calls=%fused_computation.73 | convolution fusion | flops 2883584 | bytes 622592 | tf_op jit(solution)/shard_map/rhij,rhj->rhi/dot_general | solution.py:64
  195.3 2.0 multiply_add_fusion
  199.0 1.7 fusion.191
  200.8 2.1 fusion.26
  206.4 24.7 %reduce-scatter.5.cloned.1.call-done = f32[256,32]{0,1:T(8,128)} async-done(((f32[1024,32]{0,1:T(8,128)}), f32[256,32]{0,1:T(8,128)}) %reduce-scatter.5.cloned.1.call-update) | async-done | bytes 32784 | tf_op jit(solution)/shard_map/reduce_scatter | solution.py:190
  232.7 1.9 scatter_fusion.1
  234.6 13.3 %all-to-all-start.1 = ((bf16[64,4,256]{2,1,0:T(4,128)(2,1)}), bf16[64,4,256]{2,1,0:T(4,128)(2,1)S(1)}, u32[]{:S(2)}, u32[]{:S(2)}) async-start(bf16[64,4,256]{2,1,0:T(4,128)(2,1)} %scatter_fusion.1), calls=%async_computation.3 | async-start | bytes 262144 | tf_op jit(solution)/shard_map/all_to_all | solution.py:306
  248.6 11.1 %all-to-all-done.1 = bf16[64,4,256]{2,1,0:T(4,128)(2,1)S(1)} async-done(((bf16[64,4,256]{2,1,0:T(4,128)(2,1)}), bf16[64,4,256]{2,1,0:T(4,128)(2,1)S(1)}, u32[]{:S(2)}, u32[]{:S(2)}) %all-to-all-start.1) | async-done | bytes 131104 | tf_op jit(solution)/shard_map/all_to_all | solution.py:306
  (260 shorter events, 51.8 us)
Async XLA Ops:
  6.5 107.0 %copy-start = (bf16[1,256,1024]{2,1,0:T(8,128)(2,1)S(1)}, bf16[1,256,1024]{2,1,0:T(8,128)(2,1)}, u32[]{:S(2)}) copy-start(bf16[1,256,1024]{2,1,0:T(8,128)(2,1)} %param.34) | copy-start | bytes 1572868
  6.5 23.8 %copy-start.3 = (bf16[1,1024,256]{2,1,0:T(8,128)(2,1)S(1)}, bf16[1,1024,256]{2,1,0:T(8,128)(2,1)}, u32[]{:S(2)}) copy-start(bf16[1,1024,256]{2,1,0:T(8,128)(2,1)} %param.31) | copy-start | bytes 1572868
  7.4 21.5 %copy-start.9 = (s32[64,8]{1,0:T(8,128)}, s32[64,8]{1,0:T(8,128)S(1)}, u32[]{:S(2)}) copy-start(s32[64,8]{1,0:T(8,128)S(1)} %reshape.364) | copy-start | bytes 6148
  10.9 28.2 %all-to-all-start = ((bf16[64,4,256]{2,1,0:T(4,128)(2,1)}), bf16[64,4,256]{2,1,0:T(4,128)(2,1)S(1)}, u32[]{:S(2)}, u32[]{:S(2)}) async-start(bf16[64,4,256]{2,1,0:T(4,128)(2,1)} %scatter_fusion), calls=%async_computation | async-start | bytes 262144 | tf_op jit(solution)/shard_map/all_to_all | solution.py:300
  27.5 110.9 %reduce-scatter.3.cloned.1.call-start = ((), (), s32[]{:S(2)}) async-start(), calls=%async_computation.4 | async-start | bytes 163840 | tf_op jit(solution)/shard_map/reduce_scatter | solution.py:190
  30.2 17.2 %copy-start.23 = (pred[8]{0:T(512)(128)(4,1)}, pred[8]{0:T(512)(128)(4,1)S(1)}, u32[]{:S(2)}) copy-start(pred[8]{0:T(512)(128)(4,1)S(1)} %get-tuple-element.17) | copy-start | bytes 28
  30.3 17.2 %copy-start.25 = (f32[1,1,256]{2,1,0:T(1,128)}, f32[1,1,256]{2,1,0:T(1,128)S(1)}, u32[]{:S(2)}) copy-start(f32[1,1,256]{2,1,0:T(1,128)S(1)} %get-tuple-element.82) | copy-start | bytes 3076
  30.3 17.2 %copy-start.27 = (f32[1,1,256]{2,1,0:T(1,128)}, f32[1,1,256]{2,1,0:T(1,128)S(1)}, u32[]{:S(2)}) copy-start(f32[1,1,256]{2,1,0:T(1,128)S(1)} %get-tuple-element.83) | copy-start | bytes 3076
  30.3 1.0 copy-start.4
  40.4 27.4 %collective-permute-start = (bf16[8,4,256]{2,0,1:T(8,128)(2,1)S(1)}, bf16[8,4,256]{2,0,1:T(8,128)(2,1)S(1)}, u32[]{:S(2)}, u32[]{:S(2)}) collective-permute-start(bf16[8,4,256]{2,0,1:T(8,128)(2,1)S(1)} %pad_maximum_fusion.3), channel_id=1, source_target_pairs={{0,1},{1,2},{2,3},{3,0},{4,5},{5,6},{6,7},{7,4},{8,9},{9,10},{10,1... | collective-permute-start | bytes 49160 | tf_op jit(solution)/shard_map/ppermute | solution.py:133
  43.8 37.9 %collective-permute-start.2 = (bf16[8,4,256]{2,0,1:T(8,128)(2,1)S(1)}, bf16[8,4,256]{2,0,1:T(8,128)(2,1)S(1)}, u32[]{:S(2)}, u32[]{:S(2)}) collective-permute-start(bf16[8,4,256]{2,0,1:T(8,128)(2,1)S(1)} %pad_maximum_fusion.3), channel_id=1, source_target_pairs={{0,3},{1,0},{2,1},{3,2},{4,7},{5,4},{6,5},{7,6},{8,11},{9,8},{10,9... | collective-permute-start | bytes 49160 | tf_op jit(solution)/shard_map/ppermute | solution.py:135
  47.5 0.8 copy-start.5
  48.4 0.8 copy-start.6
  49.1 16.0 %copy-start.47 = (bf16[1,96,256]{2,1,0:T(8,128)(2,1)S(1)}, bf16[1,96,256]{2,1,0:T(8,128)(2,1)}, u32[]{:S(2)}) copy-start(bf16[1,96,256]{2,1,0:T(8,128)(2,1)} %param.36) | copy-start | bytes 147460
  66.0 0.8 copy-start.45
  67.7 14.0 %collective-permute-start.1 = (bf16[8,4,256]{2,0,1:T(8,128)(2,1)S(1)}, bf16[8,4,256]{2,0,1:T(8,128)(2,1)S(1)}, u32[]{:S(2)}, u32[]{:S(2)}) collective-permute-start(bf16[8,4,256]{2,0,1:T(8,128)(2,1)S(1)} %collective-permute-done), channel_id=1, source_target_pairs={{0,1},{1,2},{2,3},{3,0},{4,5},{5,6},{6,7},{7,4},{8,9},{9,10},{10,1... | collective-permute-start | bytes 49160 | tf_op jit(solution)/shard_map/ppermute | solution.py:133
  81.9 1.1 copy-start.2
  84.5 3.7 %copy-start.1 = (f32[1,8,4,64,64]{4,3,2,1,0:T(8,128)S(1)}, f32[1,8,4,64,64]{4,3,2,1,0:T(8,128)}, u32[]{:S(2)}) copy-start(f32[1,8,4,64,64]{4,3,2,1,0:T(8,128)} %param.28) | copy-start | bytes 1572868
  88.9 1.7 copy-start.12
  88.9 1.7 copy-start.20
  103.8 2.0 copy-start.13
  107.6 1.8 copy-start.18
  114.4 116.8 %reduce-scatter.5.cloned.1.call-start = ((), (), s32[]{:S(2)}) async-start(), calls=%async_computation.5 | async-start | bytes 163840 | tf_op jit(solution)/shard_map/reduce_scatter | solution.py:190
  139.2 2.1 collective-permute-start.3
  141.4 7.3 %copy-start.26 = (f32[1,1,256]{2,1,0:T(1,128)S(1)}, f32[1,1,256]{2,1,0:T(1,128)}, u32[]{:S(2)}) copy-start(f32[1,1,256]{2,1,0:T(1,128)} %copy-done.25) | copy-start | bytes 3076
  141.4 7.3 %copy-start.28 = (f32[1,1,256]{2,1,0:T(1,128)S(1)}, f32[1,1,256]{2,1,0:T(1,128)}, u32[]{:S(2)}) copy-start(f32[1,1,256]{2,1,0:T(1,128)} %copy-done.27) | copy-start | bytes 3076
  141.4 24.8 %collective-permute-start.4 = (bf16[8,4,256]{2,0,1:T(8,128)(2,1)S(1)}, bf16[8,4,256]{2,0,1:T(8,128)(2,1)S(1)}, u32[]{:S(2)}, u32[]{:S(2)}) collective-permute-start(bf16[8,4,256]{2,0,1:T(8,128)(2,1)S(1)} %pad_maximum_fusion.2), channel_id=1, source_target_pairs={{0,1},{1,2},{2,3},{3,0},{4,5},{5,6},{6,7},{7,4},{8,9},{9,10},{10,1... | collective-permute-start | bytes 49160 | tf_op jit(solution)/shard_map/ppermute | solution.py:133
  143.6 37.2 %collective-permute-start.6 = (bf16[8,4,256]{2,0,1:T(8,128)(2,1)S(1)}, bf16[8,4,256]{2,0,1:T(8,128)(2,1)S(1)}, u32[]{:S(2)}, u32[]{:S(2)}) collective-permute-start(bf16[8,4,256]{2,0,1:T(8,128)(2,1)S(1)} %pad_maximum_fusion.2), channel_id=1, source_target_pairs={{0,3},{1,0},{2,1},{3,2},{4,7},{5,4},{6,5},{7,6},{8,11},{9,8},{10,9... | collective-permute-start | bytes 49160 | tf_op jit(solution)/shard_map/ppermute | solution.py:135
  148.9 0.8 copy-start.7
  149.7 14.6 %copy-start.46 = (bf16[1,96,256]{2,1,0:T(8,128)(2,1)S(1)}, bf16[1,96,256]{2,1,0:T(8,128)(2,1)}, u32[]{:S(2)}) copy-start(bf16[1,96,256]{2,1,0:T(8,128)(2,1)} %param.38) | copy-start | bytes 147460
  166.2 14.5 %collective-permute-start.5 = (bf16[8,4,256]{2,0,1:T(8,128)(2,1)S(1)}, bf16[8,4,256]{2,0,1:T(8,128)(2,1)S(1)}, u32[]{:S(2)}, u32[]{:S(2)}) collective-permute-start(bf16[8,4,256]{2,0,1:T(8,128)(2,1)S(1)} %collective-permute-done.4), channel_id=1, source_target_pairs={{0,1},{1,2},{2,3},{3,0},{4,5},{5,6},{6,7},{7,4},{8,9},{9,10},{10,1... | collective-permute-start | bytes 49160 | tf_op jit(solution)/shard_map/ppermute | solution.py:133
  234.6 25.1 %all-to-all-start.1 = ((bf16[64,4,256]{2,1,0:T(4,128)(2,1)}), bf16[64,4,256]{2,1,0:T(4,128)(2,1)S(1)}, u32[]{:S(2)}, u32[]{:S(2)}) async-start(bf16[64,4,256]{2,1,0:T(4,128)(2,1)} %scatter_fusion.1), calls=%async_computation.3 | async-start | bytes 262144 | tf_op jit(solution)/shard_map/all_to_all | solution.py:306
  (33 other events, 22.5 us)
Sparse Core Ops, SparseCore 0:
  114.5 23.7 reduce-scatter.2
  204.6 26.5 reduce-scatter.4
